TPU v7x, 256 devices: a whole 4x4x8 slice. The times are simulated.
256 devices in a mesh: req: 64 (over z, x, core), kv: 4 (over y).
Axes of the slice: x: 4, y: 4, z: 8, core: 2. Of those that a mesh axis runs over, the one named last changes fastest.
Arguments:
- residual_in: bfloat16 [128, 2560], P('req', 'kv'), may hold values from -8 to 8
- queries: bfloat16 [128, 2560], P('req', 'kv'), may hold values from -480 to 480
- fresh_token_keys: bfloat16 [128, 512], P('req', 'kv'), may hold values from -6 to 6
- fresh_token_values: bfloat16 [128, 512], P('req', 'kv'), may hold values from -6 to 6
- cached_key_slots: bfloat16 [128, 4096, 512], P('req', None, 'kv'), may hold values from -6 to 6
- cached_value_slots: bfloat16 [128, 4096, 512], P('req', None, 'kv'), may hold values from -6 to 6
- lengths: int32 [128], replicated, may hold values from 1 to 4096, as said below
- slot_order: int32 [128], replicated, may hold values from 0 to 127, as said below
- out_proj: bfloat16 [2560, 2560], P('kv'), may hold values from -0.5 to 0.5
- norm_gain: bfloat16 [2560], P('kv'), may hold values from 0.5 to 1.5
- expert_ids: int32 [128, 6], replicated, may hold values from 0 to 63, all different within a row; in each aligned block of 128 rows (0 to 127, 128 to 255, ...) at most 24 rows name the same one
- gate_values: float32 [128, 6], replicated, may hold values from 0.1 to 0.5
- gate_proj: bfloat16 [64, 2560, 1536], P('req', None, 'kv'), may hold values from -0.125 to 0.125
- up_proj: bfloat16 [64, 2560, 1536], P('req', None, 'kv'), may hold values from -0.125 to 0.125
- down_proj: bfloat16 [64, 1536, 2560], P('req', 'kv'), may hold values from -0.15625 to 0.15625
Outputs:
- layer_out: bfloat16 [128, 2560], P('req', 'kv')
Inputs may be any that keep to these rules, and one draw needn't show every extreme that they name: `lengths`: each request's count of cached positions; some request has exactly 4096. A permutation of the requests: slot s serves request slot_order[s], and cached_key_slots[s], cached_value_slots[s] hold that request's cache. Requests sorted by decreasing length are dealt to the 64 groups of 2 consecutive slots, one round forward, the next backward. `expert_ids`: each token names 6 different experts; no expert is named by more than 24 tokens, a bound that some block reaches.
All inputs are finite; a program needn't handle non-finite values.
Results may differ from a plain program's by a relative error of at most 0.012.
Values may be sent and summed in bfloat16 or wider, within the bound.
No kernel may reach another device: no remote copies, remote signals or barrier semaphores. Data moves between devices by JAX's collectives and lax.ppermute only.
A program may use at most 64 MiB of HBM per device.

v0:
```python
import math
import jax
import jax.numpy as jnp
from jax import lax
from jax.sharding import PartitionSpec as P


def device_blocks(term, groups, parts):
    row_count = term.shape[0] // groups
    col_count = term.shape[1] // parts
    return (
        term.reshape(groups, row_count, parts, col_count)
        .transpose(0, 2, 1, 3)
        .reshape(groups * parts * row_count, col_count)
    )


def per_device(
    residual_in,
    queries,
    fresh_token_keys,
    fresh_token_values,
    cached_key_slots,
    cached_value_slots,
    lengths,
    slot_order,
    out_proj,
    norm_gain,
    expert_ids,
    gate_values,
    gate_proj,
    up_proj,
    down_proj,
):
    req_count = lax.axis_size("req")
    kv_count = lax.axis_size("kv")
    req_index = lax.axis_index("req")
    per_dev = residual_in.shape[0]
    head_dim = fresh_token_keys.shape[1]
    total_reqs = lengths.shape[0]
    model_width = out_proj.shape[1]
    all_queries, all_keys, all_values = (
        lax.all_gather(queries, "req", axis=0, tiled=True),
        lax.all_gather(fresh_token_keys, "req", axis=0, tiled=True),
        lax.all_gather(fresh_token_values, "req", axis=0, tiled=True),
    )
    served = lax.dynamic_slice_in_dim(slot_order, req_index * per_dev, per_dev)
    query_rows = all_queries[served].reshape(per_dev, -1, head_dim)
    self_key_row = all_keys[served]
    self_value_row = all_values[served]
    live_len = lengths[served]
    inv_root = 1.0 / math.sqrt(head_dim)
    scores = (
        jnp.einsum("rqd,rld->rql", query_rows, cached_key_slots, preferred_element_type=jnp.float32)
        * inv_root
    )
    positions = jnp.arange(cached_key_slots.shape[1])
    scores = jnp.where((positions[None, :] < live_len[:, None])[:, None, :], scores, -1e30)
    own_score = (
        jnp.einsum("rqd,rd->rq", query_rows, self_key_row, preferred_element_type=jnp.float32)
        * inv_root
    )
    highest = jnp.maximum(jnp.max(scores, axis=2), own_score)
    weights = jnp.exp(scores - highest[:, :, None])
    own_weight = jnp.exp(own_score - highest)
    totals = jnp.sum(weights, axis=2) + own_weight
    numerator = jnp.einsum(
        "rql,rld->rqd",
        weights.astype(jnp.bfloat16),
        cached_value_slots,
        preferred_element_type=jnp.float32,
    )
    own_low = lax.optimization_barrier(own_weight.astype(jnp.bfloat16)).astype(jnp.float32)
    numerator = numerator + own_low[:, :, None] * self_value_row.astype(jnp.float32)[:, None, :]
    attended = (numerator / totals[:, :, None]).astype(jnp.bfloat16).reshape(per_dev, -1)
    projected = jnp.dot(attended, out_proj, preferred_element_type=jnp.float32)
    placed = jnp.zeros((total_reqs, model_width), jnp.float32).at[served].set(projected)
    attn_part = lax.psum_scatter(
        device_blocks(placed, req_count, kv_count), ("req", "kv"), scatter_dimension=0, tiled=True
    )
    hidden = residual_in.astype(jnp.float32) + attn_part
    squares = lax.psum(jnp.sum(hidden * hidden, axis=1), "kv")
    normed = (
        hidden * lax.rsqrt(squares / model_width + 1e-06)[:, None] * norm_gain.astype(jnp.float32)
    ).astype(jnp.bfloat16)
    gathered = lax.all_gather(normed, ("req", "kv"), axis=0, tiled=True)
    tokens = (
        gathered.reshape(req_count, kv_count, per_dev, -1)
        .transpose(0, 2, 1, 3)
        .reshape(total_reqs, -1)
    )
    local_count = gate_proj.shape[0]
    capacity = min(2 * total_reqs * expert_ids.shape[1] // (local_count * req_count), total_reqs)
    expert = req_index * local_count + 0
    named_here = expert_ids == expert
    token_gate = jnp.sum(jnp.where(named_here, gate_values, 0.0), axis=1)
    uses_expert = jnp.any(named_here, axis=1)
    picked = jnp.nonzero(uses_expert, size=capacity, fill_value=0)[0].astype(jnp.int32)
    valid_rows = jnp.arange(capacity) < jnp.sum(uses_expert.astype(jnp.int32))
    row_block = tokens[picked]
    gate_h = jnp.dot(row_block, gate_proj[0], preferred_element_type=jnp.float32)
    up_h = jnp.dot(row_block, up_proj[0], preferred_element_type=jnp.float32)
    inner_act = (jax.nn.silu(gate_h) * up_h).astype(jnp.bfloat16)
    outputs = jnp.dot(inner_act, down_proj[0], preferred_element_type=jnp.float32)
    row_gate = jnp.where(valid_rows, token_gate[picked], 0.0)
    weighted_list = [outputs * row_gate[:, None]]
    picked_list = [picked]
    stacked_rows = jnp.concatenate(weighted_list, axis=0)
    stacked_idx = jnp.concatenate(picked_list, axis=0)
    mixture = jnp.zeros((total_reqs, model_width), jnp.float32).at[stacked_idx].add(stacked_rows)
    moe_part = lax.psum_scatter(
        device_blocks(mixture, req_count, kv_count), ("req", "kv"), scatter_dimension=0, tiled=True
    )
    return (hidden + moe_part).astype(jnp.bfloat16)


def solution(mesh):
    in_specs = (
        P("req", "kv"),
        P("req", "kv"),
        P("req", "kv"),
        P("req", "kv"),
        P("req", None, "kv"),
        P("req", None, "kv"),
        P(),
        P(),
        P("kv", None),
        P("kv"),
        P(),
        P(),
        P("req", None, "kv"),
        P("req", None, "kv"),
        P("req", "kv", None),
    )
    out_specs = P("req", "kv")
    return jax.shard_map(
        per_device, mesh=mesh, in_specs=in_specs, out_specs=out_specs, check_vma=False
    )
```

profile of v0, /device:TPU:2, one launch (start us, length us, event | category | flops | bytes accessed | tf_op | source)
XLA Modules:
  0.0 775.9 jit_solution(7634944071850056132)
XLA Ops:
  6.5 0.9 compare_select_fusion.2
  7.4 1.4 gather_fusion
  8.8 0.1 iota_compare_fusion
  8.9 42.3 %all-gather.1 = bf16[64,2,128]{2,1,0:T(2,128)(2,1)S(1)} all-gather(bf16[1,2,128]{2,1,0:T(2,128)(2,1)} %bitcast.58), channel_id=1, replica_groups=mesh['req'=64,'kv'=4] {'req'}, dimensions={0}, use_global_device_ids=true | all-gather | bytes 33280 | tf_op jit(solution)/shard_map/all_gather | solution.py:44
  51.3 0.6 gather_fusion.2
  51.8 37.5 %all-gather.2 = bf16[64,2,128]{2,1,0:T(2,128)(2,1)S(1)} all-gather(bf16[1,2,128]{2,1,0:T(2,128)(2,1)} %bitcast.59), channel_id=1, replica_groups=mesh['req'=64,'kv'=4] {'req'}, dimensions={0}, use_global_device_ids=true | all-gather | bytes 33280 | tf_op jit(solution)/shard_map/all_gather | solution.py:45
  89.3 0.6 gather_fusion.3
  89.9 41.7 %all-gather = bf16[64,2,640]{2,1,0:T(2,128)(2,1)S(1)} all-gather(bf16[1,2,640]{2,1,0:T(2,128)(2,1)} %bitcast.57), channel_id=1, replica_groups=mesh['req'=64,'kv'=4] {'req'}, dimensions={0}, use_global_device_ids=true | all-gather | bytes 166400 | tf_op jit(solution)/shard_map/all_gather | solution.py:43
  131.6 0.7 reshape.239
  132.3 1.5 gather_fusion.1
  133.8 0.1 fusion.40
  134.0 2.4 fusion.47
  136.4 0.2 fusion.21
  136.7 0.4 fusion.16
  137.1 0.0 copy-done
  137.1 0.5 fusion.36
  137.6 1.8 scatter_custom_fusion
  139.4 2.7 reshape.153
  142.1 3.1 copy.27
  145.2 3.1 reshape.154
  148.3 0.0 all-reduce.5.cloned.1.call-update
  148.3 0.0 all-reduce.7.cloned.1.call-start
  148.4 0.1 copy.28
  148.5 0.2 reduce-window.6
  148.7 0.1 fusion.25
  148.8 1.4 scatter_custom_fusion.1
  150.3 0.1 copy.29
  150.4 0.6 convert_reduce_fusion
  151.0 0.8 fusion.34
  151.8 0.7 gather_fusion.5
  152.5 0.7 compare_select_fusion.3
  153.2 255.0 %all-reduce.5.cloned.1.call-done = f32[512,640]{1,0:T(8,128)} async-done(((f32[512,640]{1,0:T(8,128)}), f32[512,640]{1,0:T(8,128)}) %all-reduce.5.cloned.1.call-update) | async-done | bytes 1310736
  408.1 0.8 multiply_reduce_fusion
  409.0 10.2 %psum.7 = f32[2]{0:T(128)S(1)} all-reduce(f32[2]{0:T(128)S(1)} %multiply_reduce_fusion), channel_id=1, replica_groups=mesh['req'=64,'kv'=4] {'kv'}, use_global_device_ids=true, to_apply=%region_10.11 | all-reduce | flops 2 | bytes 16 | tf_op jit(solution)/shard_map/psum | solution.py:82
  419.2 0.8 fusion.39
  420.0 70.2 %all-gather.3 = bf16[256,2,640]{2,1,0:T(2,128)(2,1)S(1)} all-gather(bf16[1,2,640]{2,1,0:T(2,128)(2,1)S(1)} %fusion.39), channel_id=1, replica_groups=mesh['req'=64,'kv'=4] {'req','kv'}, dimensions={0}, use_global_device_ids=true | all-gather | bytes 657920 | tf_op jit(solution)/shard_map/all_gather | solution.py:86
  490.2 0.3 copy.30
  490.5 0.9 copy.35
  491.4 1.9 gather_fusion.4
  493.3 1.9 fusion.4
  495.2 3.8 convolution_multiply_fusion.1
  499.0 2.5 scatter_custom_fusion.2
  501.5 2.7 reshape.158
  504.2 3.1 copy.31
  507.3 3.1 reshape.159
  510.3 0.0 all-reduce.7.cloned.1.call-update
  510.3 257.4 %all-reduce.7.cloned.1.call-done = f32[512,640]{1,0:T(8,128)} async-done(((f32[512,640]{1,0:T(8,128)}), f32[512,640]{1,0:T(8,128)}) %all-reduce.7.cloned.1.call-update) | async-done | bytes 1310736
  767.7 1.3 fusion.35
  (26 shorter events, 0.2 us)
Async XLA Ops:
  6.5 130.6 %copy-start = (bf16[640,2560]{1,0:T(8,128)(2,1)S(1)}, bf16[640,2560]{1,0:T(8,128)(2,1)}, u32[]{:S(2)}) copy-start(bf16[640,2560]{1,0:T(8,128)(2,1)} %param.23) | copy-start | bytes 9830404
  6.5 401.6 %all-reduce.5.cloned.1.call-start = ((), (), s32[]{:S(2)}) async-start(), calls=%async_computation | async-start | bytes 2621440
  133.8 2.8 copy-start.1
  145.2 3.2 copy-start.3
  145.2 3.2 copy-start.4
  145.2 263.0 %copy-start.2 = (bf16[2,640]{1,0:T(2,128)(2,1)S(1)}, bf16[2,640]{1,0:T(2,128)(2,1)}, u32[]{:S(2)}) copy-start(bf16[2,640]{1,0:T(2,128)(2,1)} %param.15) | copy-start | bytes 7684
  145.2 263.8 %copy-start.5 = (bf16[640]{0:T(1024)(128)(2,1)S(1)}, bf16[640]{0:T(1024)(128)(2,1)}, u32[]{:S(2)}) copy-start(bf16[640]{0:T(1024)(128)(2,1)} %param.24) | copy-start | bytes 3844
  148.3 619.4 %all-reduce.7.cloned.1.call-start = ((), (), s32[]{:S(2)}) async-start(), calls=%async_computation.1 | async-start | bytes 2621440
Sparse Core Ops, SparseCore 0:
  148.4 259.6 all-reduce.4
  510.5 257.1 all-reduce.6
where the time goes:
time: 777 us; the launch traced here: 776 us
  waiting for transfers between devices  512 us (66%)
  blocking collectives  202 us (26%)
  local copies, waits for them, and re-layouts  28.2 us (4%)
  between operations  13.5 us (2%)
  other arithmetic  10.5 us (1%)
  matrix products  9.24 us (1%)
    unnamed x4, waiting for transfers between devices  512 us
    all_gather x1, blocking collectives, per_device(): gathered = lax.all_gather(normed, ('req', 'kv'), axis=0, tiled=True)  70.2 us
    all_gather x1, blocking collectives, per_device(): lax.all_gather(fresh_token_keys, 'req', axis=0, tiled=True)  42.3 us
    all_gather x1, blocking collectives, per_device(): lax.all_gather(queries, 'req', axis=0, tiled=True)  41.7 us
    all_gather x1, blocking collectives, per_device(): lax.all_gather(fresh_token_values, 'req', axis=0, tiled=True)  37.5 us
  transfers between devices with their start and end apart: 2, of which 2 were waited for; matrix products, arithmetic and copies ran while one was open for 1% of the time, Pallas kernels for 0%

commit v1 on v0

--- a/solution.py
+++ b/solution.py
@@ -39,8 +39,14 @@
     head_dim = fresh_token_keys.shape[1]
     total_reqs = lengths.shape[0]
     model_width = out_proj.shape[1]
+
+    def point_array(page):
+        return jnp.concatenate(
+            lax.all_to_all(jnp.stack([page] * lax.psum(1, "req")), "req", 0, 0), axis=0
+        )
+
     all_queries, all_keys, all_values = (
-        lax.all_gather(queries, "req", axis=0, tiled=True),
+        point_array(queries),
         lax.all_gather(fresh_token_keys, "req", axis=0, tiled=True),
         lax.all_gather(fresh_token_values, "req", axis=0, tiled=True),
     )

time: 777 us -> 748 us (0.963)
  blocking collectives: 202 us -> 159 us
  starting transfers between devices: 0.04 us -> 12.1 us
    all_gather x1 -> x0, blocking collectives: 41.7 us -> none  [per_device(): lax.all_gather(queries, 'req', axis=0, tiled=True)]
    all_to_all x0 -> x1, starting transfers between devices: none -> 12 us  [point_array(): lax.all_to_all(jnp.stack([page] * lax.psum(1, 'req')), 'req', 0, 0)]
  transfers between devices with their start and end apart: 2 -> 3, of which waited for: 2 -> 2; matrix products, arithmetic and copies ran while one was open for 1% -> 1% of each run, Pallas kernels for 0% -> 0%
where the time goes in v1:
time: 748 us; the launch traced here: 747 us
  waiting for transfers between devices  512 us (68%)
  blocking collectives  159 us (21%)
  local copies, waits for them, and re-layouts  30.3 us (4%)
  between operations  13.5 us (2%)
  starting transfers between devices  12.1 us (2%)
  other arithmetic  11.9 us (2%)
  matrix products  9.24 us (1%)
    unnamed x4, waiting for transfers between devices  512 us
    all_gather x1, blocking collectives, per_device(): gathered = lax.all_gather(normed, ('req', 'kv'), axis=0, tiled=True)  70.2 us
    all_gather x1, blocking collectives, per_device(): lax.all_gather(fresh_token_keys, 'req', axis=0, tiled=True)  40.6 us
    all_gather x1, blocking collectives, per_device(): lax.all_gather(fresh_token_values, 'req', axis=0, tiled=True)  37.5 us
  transfers between devices with their start and end apart: 3, of which 2 were waited for; matrix products, arithmetic and copies ran while one was open for 1% of the time, Pallas kernels for 0%

profile of v1, /device:TPU:2, one launch (start us, length us, event | category | flops | bytes accessed | tf_op | source)
XLA Modules:
  0.0 747.5 jit_solution(17851977969031239512)
XLA Ops:
  6.5 1.6 stack.2
  8.1 12.0 %all-to-all-start = ((bf16[64,2,640]{2,1,0:T(2,128)(2,1)}), bf16[64,2,640]{2,1,0:T(2,128)(2,1)S(1)}, u32[]{:S(2)}, u32[]{:S(2)}) async-start(bf16[64,2,640]{2,1,0:T(2,128)(2,1)} %stack.2), calls=%async_computation | async-start | bytes 327680 | tf_op jit(solution)/shard_map/all_to_all | solution.py:45
  20.1 0.0 all-reduce.5.cloned.1.call-start
  20.2 0.7 compare_select_fusion.2
  20.9 1.3 gather_fusion
  22.2 0.1 iota_compare_fusion
  22.3 0.7 select_reduce_fusion
  23.0 40.6 %all-gather = bf16[64,2,128]{2,1,0:T(2,128)(2,1)S(1)} all-gather(bf16[1,2,128]{2,1,0:T(2,128)(2,1)} %bitcast.56), channel_id=1, replica_groups=mesh['req'=64,'kv'=4] {'req'}, dimensions={0}, use_global_device_ids=true | all-gather | bytes 33280 | tf_op jit(solution)/shard_map/all_gather | solution.py:50
  63.7 0.6 gather_fusion.2
  64.2 37.5 %all-gather.1 = bf16[64,2,128]{2,1,0:T(2,128)(2,1)S(1)} all-gather(bf16[1,2,128]{2,1,0:T(2,128)(2,1)} %bitcast.57), channel_id=1, replica_groups=mesh['req'=64,'kv'=4] {'req'}, dimensions={0}, use_global_device_ids=true | all-gather | bytes 33280 | tf_op jit(solution)/shard_map/all_gather | solution.py:51
  101.7 0.6 gather_fusion.3
  102.3 0.7 copy.28
  103.1 1.0 reduce-window.6
  104.1 0.7 reshape.156
  104.8 1.5 gather_fusion.1
  106.3 0.1 fusion.40
  106.4 2.4 fusion.47
  108.9 0.2 fusion.21
  109.1 0.4 fusion.16
  109.6 0.5 fusion.36
  110.1 1.8 scatter_custom_fusion
  111.9 2.7 reshape.159
  114.6 3.1 copy.27
  117.6 3.1 reshape.160
  120.7 0.0 all-reduce.7.cloned.1.call-start
  120.8 0.1 fusion.25
  120.9 1.4 scatter_custom_fusion.1
  122.3 0.1 copy.29
  122.5 0.6 convert_reduce_fusion
  123.1 0.8 fusion.34
  123.9 0.7 gather_fusion.5
  124.6 0.7 compare_select_fusion.3
  125.2 254.5 %all-reduce.5.cloned.1.call-done = f32[512,640]{1,0:T(8,128)} async-done(((f32[512,640]{1,0:T(8,128)}), f32[512,640]{1,0:T(8,128)}) %all-reduce.5.cloned.1.call-update) | async-done | bytes 1310736
  379.7 0.8 multiply_reduce_fusion
  380.6 10.2 %psum.7 = f32[2]{0:T(128)S(1)} all-reduce(f32[2]{0:T(128)S(1)} %multiply_reduce_fusion), channel_id=1, replica_groups=mesh['req'=64,'kv'=4] {'kv'}, use_global_device_ids=true, to_apply=%region_10.11 | all-reduce | flops 2 | bytes 16 | tf_op jit(solution)/shard_map/psum | solution.py:88
  390.8 0.8 fusion.39
  391.6 70.2 %all-gather.2 = bf16[256,2,640]{2,1,0:T(2,128)(2,1)S(1)} all-gather(bf16[1,2,640]{2,1,0:T(2,128)(2,1)S(1)} %fusion.39), channel_id=1, replica_groups=mesh['req'=64,'kv'=4] {'req','kv'}, dimensions={0}, use_global_device_ids=true | all-gather | bytes 657920 | tf_op jit(solution)/shard_map/all_gather | solution.py:92
  461.8 0.3 copy.30
  462.0 0.9 copy.35
  463.0 1.9 gather_fusion.4
  464.9 1.9 fusion.4
  466.8 3.8 convolution_multiply_fusion.1
  470.6 2.5 scatter_custom_fusion.2
  473.1 2.7 reshape.164
  475.8 3.1 copy.31
  478.9 3.1 reshape.165
  481.9 257.4 %all-reduce.7.cloned.1.call-done = f32[512,640]{1,0:T(8,128)} async-done(((f32[512,640]{1,0:T(8,128)}), f32[512,640]{1,0:T(8,128)}) %all-reduce.7.cloned.1.call-update) | async-done | bytes 1310736
  739.3 1.3 fusion.35
  (24 shorter events, 0.2 us)
Async XLA Ops:
  6.5 103.0 %copy-start = (bf16[640,2560]{1,0:T(8,128)(2,1)S(1)}, bf16[640,2560]{1,0:T(8,128)(2,1)}, u32[]{:S(2)}) copy-start(bf16[640,2560]{1,0:T(8,128)(2,1)} %param.23) | copy-start | bytes 9830404
  8.1 96.0 %all-to-all-start = ((bf16[64,2,640]{2,1,0:T(2,128)(2,1)}), bf16[64,2,640]{2,1,0:T(2,128)(2,1)S(1)}, u32[]{:S(2)}, u32[]{:S(2)}) async-start(bf16[64,2,640]{2,1,0:T(2,128)(2,1)} %stack.2), calls=%async_computation | async-start | bytes 327680 | tf_op jit(solution)/shard_map/all_to_all | solution.py:45
  20.1 359.6 %all-reduce.5.cloned.1.call-start = ((), (), s32[]{:S(2)}) async-start(), calls=%async_computation.1 | async-start | bytes 2621440
  106.3 2.8 copy-start.1
  117.6 262.1 %copy-start.2 = (bf16[2,640]{1,0:T(2,128)(2,1)S(1)}, bf16[2,640]{1,0:T(2,128)(2,1)}, u32[]{:S(2)}) copy-start(bf16[2,640]{1,0:T(2,128)(2,1)} %param.15) | copy-start | bytes 7684
  117.6 262.9 %copy-start.3 = (bf16[640]{0:T(1024)(128)(2,1)S(1)}, bf16[640]{0:T(1024)(128)(2,1)}, u32[]{:S(2)}) copy-start(bf16[640]{0:T(1024)(128)(2,1)} %param.24) | copy-start | bytes 3844
  120.7 618.6 %all-reduce.7.cloned.1.call-start = ((), (), s32[]{:S(2)}) async-start(), calls=%async_computation.2 | async-start | bytes 2621440
Sparse Core Ops, SparseCore 0:
  120.9 258.8 all-reduce.4
  482.1 257.1 all-reduce.6
